TPU v7x, 256 devices: a whole 4x4x8 slice. The times are simulated.
256 devices in a mesh: pair: 2 (over core), seq: 32 (over y, x, z_hi), tp: 4 (over z_lo).
Axes of the slice: x: 4, y: 4, z: 8 (z_hi: 2, z_lo: 4; z = z_hi * 4 + z_lo), core: 2. Of those that a mesh axis runs over, the one named last changes fastest.
Arguments:
- hidden: bfloat16 [36864, 3072], P(('pair', 'seq'), 'tp'), may hold values from -11 to 11
- positions: int32 [3, 36864], P(None, ('pair', 'seq')), may hold values from 0 to 63, as said below
- lengths: int32 [8], P('pair'), may hold values from 1 to 512, as said below
- step_index: int32 [1], replicated, may hold values from 0 to 7
- layer_mod: float32 [8, 3, 3072], P('pair'), may hold values from -3 to 3
- final_mod: float32 [8, 2, 3072], P('pair'), may hold values from -3 to 3
- qkv_weight: bfloat16 [3072, 3, 1536], P(None, None, 'tp'), may hold values from -0.108253175 to 0.108253175
- q_gain: float32 [128], replicated, may hold values from 0.5 to 5.5
- k_gain: float32 [128], replicated, may hold values from 0.5 to 5.5
- out_weight: bfloat16 [1536, 3072], P('tp'), may hold values from -0.15625 to 0.15625
- final_weight: bfloat16 [3072, 64], P('tp'), may hold values from -0.109375 to 0.109375
- latents: float32 [16384, 64], P(('pair', 'seq')), may hold values from -6 to 6
Outputs:
- new_hidden: bfloat16 [36864, 3072], P(('pair', 'seq'), 'tp')
- attention_lse: float32 [12, 36864], P('tp', ('pair', 'seq'))
- next_latents: float32 [16384, 64], P(('pair', 'seq'))
Inputs may be any that keep to these rules, and one draw needn't show every extreme that they name: `lengths`: some sequence has all 512 text tokens live and some sequence just one. `positions`: the first component is zero; text rows are zero; the image rows of a sequence hold each cell (row, column) of a grid 64 cells wide exactly once, the same for both sequences of a prompt.
All inputs are finite; a program needn't handle non-finite values.
Results may differ from a plain program's by a relative error of at most 0.01.
Values may be sent and summed in bfloat16 or wider, within the bound.
No kernel may reach another device: no remote copies, remote signals or barrier semaphores. Data moves between devices by JAX's collectives and lax.ppermute only.
A program may use at most 128 MiB of HBM per device.

v0:
```python
import jax
import jax.numpy as jnp
from jax import lax
from jax.sharding import PartitionSpec as P

ROPE_T = 16
ROPE_H = 56
ROPE_W = 56
STEPS = 8
IMG_DEV = 512
TXT_DEV = 64
GUIDE = 3.5
SHIFT = 3.0


def swapped(block, axis, bit):
    count = lax.axis_size(axis)
    route = []
    for low in range(count):
        high = low | 1 << bit
        if high != low and high < count:
            route += [(low, high), (high, low)]
    return lax.ppermute(block, axis, route)


def rope_angles(ids_block):
    angle_parts = []
    for axis_pos, rope_width in ((0, ROPE_T), (1, ROPE_H), (2, ROPE_W)):
        frequencies = 10000.0 ** (-jnp.arange(0, rope_width, 2).astype(jnp.float32) / rope_width)
        angle_parts.append(ids_block[axis_pos].astype(jnp.float32)[:, None] * frequencies[None, :])
    angles = jnp.concatenate(angle_parts, axis=1)
    return (jnp.cos(angles), jnp.sin(angles))


def rotate(tensor, cosine, sine_part):
    dims_in = tensor.shape
    pair_view = tensor.reshape(dims_in[0], dims_in[1], dims_in[2] // 2, 2)
    first_part = pair_view[..., 0]
    second_part = pair_view[..., 1]
    cosine = cosine[:, None, :]
    sine_part = sine_part[:, None, :]
    turned = jnp.stack(
        [
            cosine * first_part - sine_part * second_part,
            sine_part * first_part + cosine * second_part,
        ],
        axis=-1,
    )
    return turned.reshape(dims_in)


def rms_gain(tensor, gain_vec):
    return tensor * lax.rsqrt(jnp.mean(tensor * tensor, axis=-1, keepdims=True) + 1e-06) * gain_vec


def modulate(features, shift_vec, scale_vec):
    row_mean = jnp.mean(features, axis=-1, keepdims=True)
    row_var = jnp.mean(features * features, axis=-1, keepdims=True) - row_mean * row_mean
    return (features - row_mean) * lax.rsqrt(row_var + 1e-06) * (1.0 + scale_vec) + shift_vec


def sigma_at(step_now):
    time_now = 1.0 - step_now.astype(jnp.float32) / STEPS
    return SHIFT * time_now / (1.0 + (SHIFT - 1.0) * time_now)


def attend_block(softmax_state, queries, packet, anchor, text_count):
    rows_dev = IMG_DEV + TXT_DEV
    piece_count = packet.shape[1] // rows_dev
    offset = jnp.arange(rows_dev, dtype=jnp.int32)
    score_scale = queries.shape[-1] ** (-0.5)

    def fold_piece(piece_idx, carried):
        row_max, row_sum, weighted = carried
        key_piece = lax.dynamic_slice_in_dim(packet, piece_idx * rows_dev, rows_dev, 1)
        text_index = (anchor + piece_idx) * TXT_DEV + offset - IMG_DEV
        is_live = (offset < IMG_DEV) | (text_index < text_count)
        scores = (
            jnp.einsum("qhd,khd->hqk", queries, key_piece[0], preferred_element_type=jnp.float32)
            * score_scale
        )
        scores = jnp.where(is_live[None, None, :], scores, -jnp.inf)
        new_max = jnp.maximum(row_max, jnp.max(scores, axis=2))
        exps = jnp.exp(scores - new_max[:, :, None])
        decay = jnp.exp(row_max - new_max)
        row_sum = row_sum * decay + jnp.sum(exps, axis=2)
        weighted = weighted * decay[:, :, None] + jnp.einsum(
            "hqk,khd->hqd",
            exps.astype(jnp.bfloat16),
            key_piece[1],
            preferred_element_type=jnp.float32,
        )
        return (new_max, row_sum, weighted)

    return lax.fori_loop(0, piece_count, fold_piece, softmax_state)


def on_device(
    hidden,
    positions,
    lengths,
    step_index,
    layer_mod,
    final_mod,
    qkv_weight,
    q_gain,
    k_gain,
    out_weight,
    final_weight,
    latents,
):
    spread = lax.axis_size("seq") // 4
    bit_count = spread.bit_length() - 1
    seq_pos = lax.axis_index("seq")
    local_seq = seq_pos // spread
    shard_pos = seq_pos % spread
    tp_pos = lax.axis_index("tp")
    local_width = hidden.shape[1]
    gathered = lax.all_gather(hidden, "tp", axis=1, tiled=True)
    model_width = gathered.shape[1]
    rows_dev = gathered.shape[0]
    layer_terms = lax.dynamic_index_in_dim(layer_mod, local_seq, 0, keepdims=False)
    text_count = lax.dynamic_index_in_dim(lengths, local_seq, 0, keepdims=False)
    modulated = modulate(gathered.astype(jnp.float32), layer_terms[0], layer_terms[1]).astype(
        jnp.bfloat16
    )
    head_dim = q_gain.shape[0]
    head_cols = qkv_weight.shape[2]
    heads_here = head_cols // head_dim
    projected = jnp.dot(
        modulated,
        qkv_weight.reshape(model_width, 3 * head_cols),
        preferred_element_type=jnp.float32,
    )
    projected = projected.reshape(rows_dev, 3, heads_here, head_dim)
    cosine, sine_part = rope_angles(positions)
    queries = rotate(rms_gain(projected[:, 0], q_gain), cosine, sine_part).astype(jnp.bfloat16)
    key_rot = rotate(rms_gain(projected[:, 1], k_gain), cosine, sine_part).astype(jnp.bfloat16)
    values = projected[:, 2].astype(jnp.bfloat16)
    packet = jnp.stack([key_rot, values])
    softmax_state = (
        jnp.full((heads_here, rows_dev), -jnp.inf, jnp.float32),
        jnp.zeros((heads_here, rows_dev), jnp.float32),
        jnp.zeros((heads_here, rows_dev, head_dim), jnp.float32),
    )
    held_keys = packet
    for bit_pos in range(bit_count):
        far_keys = swapped(held_keys, "seq", bit_pos)
        block_size = 1 << bit_pos
        lower_half = shard_pos // block_size % 2 == 0
        held_keys = jnp.where(
            lower_half,
            jnp.concatenate([held_keys, far_keys], axis=1),
            jnp.concatenate([far_keys, held_keys], axis=1),
        )
    softmax_state = attend_block(softmax_state, queries, held_keys, 0, text_count)
    row_max, row_sum, weighted = softmax_state
    attended = (weighted / row_sum[:, :, None]).astype(jnp.bfloat16)
    log_sums = row_max + jnp.log(row_sum)
    attn_flat = attended.transpose(1, 0, 2).reshape(rows_dev, head_cols)
    partial_out = jnp.dot(attn_flat, out_weight, preferred_element_type=jnp.float32)
    update = lax.psum_scatter(
        partial_out.astype(jnp.bfloat16), "tp", scatter_dimension=1, tiled=True
    ).astype(jnp.float32)
    gate_slice = lax.dynamic_slice_in_dim(layer_terms[2], tp_pos * local_width, local_width, 0)
    new_hidden = (hidden.astype(jnp.float32) + gate_slice * update).astype(jnp.bfloat16)
    final_terms = lax.dynamic_index_in_dim(final_mod, local_seq, 0, keepdims=False)
    final_shift = lax.dynamic_slice_in_dim(final_terms[0], tp_pos * local_width, local_width, 0)
    final_scale = lax.dynamic_slice_in_dim(final_terms[1], tp_pos * local_width, local_width, 0)
    image_rows = new_hidden[:IMG_DEV].astype(jnp.float32)
    weight = final_weight.astype(jnp.float32)
    row_sums = jnp.sum(image_rows, axis=1)
    squares = jnp.sum(image_rows * image_rows, axis=1)
    row_sums, squares = lax.psum((row_sums, squares), "tp")
    row_mean = row_sums / model_width
    inv_std = lax.rsqrt(squares / model_width - row_mean * row_mean + 1e-06)
    final_in = (image_rows - row_mean[:, None]) * inv_std[:, None] * (
        1.0 + final_scale
    ) + final_shift
    velocity = lax.psum(
        jnp.dot(final_in, weight, precision=lax.Precision.HIGHEST).astype(jnp.bfloat16), "tp"
    ).astype(jnp.float32)
    half_rows = IMG_DEV // 2
    is_cond = local_seq % 2 == 0
    outgoing = jnp.where(is_cond, velocity[half_rows:], velocity[:half_rows])
    partner_half = swapped(outgoing.astype(jnp.bfloat16), "seq", bit_count).astype(outgoing.dtype)
    own_half = jnp.where(is_cond, velocity[:half_rows], velocity[half_rows:])
    cond_vel = jnp.where(is_cond, own_half, partner_half)
    uncond_vel = jnp.where(is_cond, partner_half, own_half)
    guided = uncond_vel + GUIDE * (cond_vel - uncond_vel)
    step_now = step_index[0]
    time_step = sigma_at(step_now + 1) - sigma_at(step_now)
    return (new_hidden, log_sums, latents + time_step * guided)


def solution(mesh):
    return jax.shard_map(
        on_device,
        mesh=mesh,
        in_specs=(
            P(("pair", "seq"), "tp"),
            P(None, ("pair", "seq")),
            P("pair"),
            P(),
            P("pair", None, None),
            P("pair", None, None),
            P(None, None, "tp"),
            P(),
            P(),
            P("tp", None),
            P("tp", None),
            P(("pair", "seq"), None),
        ),
        out_specs=(P(("pair", "seq"), "tp"), P("tp", ("pair", "seq")), P(("pair", "seq"), None)),
        check_vma=False,
    )
```

profile of v0, /device:TPU:2, one launch (start us, length us, event | category | flops | bytes accessed | tf_op | source)
XLA Modules:
  0.0 560.9 jit_solution(13021237416934958148)
XLA Ops:
  8.0 10.3 %copy.17 = bf16[3072,3,384]{0,2,1:T(8,128)(2,1)} copy(bf16[3072,3,384]{2,0,1:T(8,128)(2,1)} %param.20) | data formatting | bytes 14155776 | tf_op args[6]
  20.3 65.6 %all-gather.2.cloned.1.call-done = bf16[576,3072]{1,0:T(8,128)(2,1)} async-done(((bf16[576,768]{1,0:T(8,128)(2,1)}), bf16[576,3072]{1,0:T(8,128)(2,1)}) %all-gather.2.cloned.1.call-update) | async-done | bytes 3538960 | tf_op jit(solution)/shard_map/all_gather | solution.py:119
  85.9 3.3 convert_reduce_fusion
  89.2 8.0 %fusion.26 = f32[576,3,3,128]{3,0,2,1:T(8,128)S(1)} fusion(bf16[3,3,128,3072]{3,2,1,0:T(8,128)(2,1)} %bitcast.68, bf16[576,3072]{1,0:T(8,128)(2,1)S(1)} %copy-done.1, f32[3072]{0:T(1024)S(1)} %bitcast.71, f32[3072]{0:T(1024)S(1)} %bitcast.70, f32[576]{0:T(1024)S(1)} %get-tuple-element.306, f32[576]{0:T(1024)S(1)} %get-tuple-element.305), kind=kOutput, calls=%fused_computation.38 | convolution fusion | flops 4087480320 | bytes 13300224 | tf_op jit(solution)/shard_map/dot_general | solution.py:130
  112.7 3.4 subtract_convert_fusion
  122.5 4.5 collective-permute-start
  127.0 30.3 %collective-permute-done = bf16[2,576,3,128]{3,1,2,0:T(8,128)(2,1)} collective-permute-done((bf16[2,576,3,128]{3,1,2,0:T(8,128)(2,1)}, bf16[2,576,3,128]{3,1,2,0:T(8,128)(2,1)}, u32[]{:S(2)}, u32[]{:S(2)}) %collective-permute-start) | collective-permute-done | bytes 884768 | tf_op jit(solution)/shard_map/ppermute | solution.py:23
  161.0 39.1 %collective-permute-done.1 = bf16[2,1152,3,128]{3,1,2,0:T(8,128)(2,1)} collective-permute-done((bf16[2,1152,3,128]{3,1,2,0:T(8,128)(2,1)}, bf16[2,1152,3,128]{3,1,2,0:T(8,128)(2,1)}, u32[]{:S(2)}, u32[]{:S(2)}) %collective-permute-start.1) | collective-permute-done | bytes 1769504 | tf_op jit(solution)/shard_map/ppermute | solution.py:23
  200.1 5.3 maximum_select_fusion.1
  211.6 71.9 %collective-permute-done.2 = bf16[2,2304,3,128]{3,1,2,0:T(8,128)(2,1)} collective-permute-done((bf16[2,2304,3,128]{3,1,2,0:T(8,128)(2,1)}, bf16[2,2304,3,128]{3,1,2,0:T(8,128)(2,1)}, u32[]{:S(2)}, u32[]{:S(2)}) %collective-permute-start.2) | collective-permute-done | bytes 3538976 | tf_op jit(solution)/shard_map/ppermute | solution.py:23
  283.5 9.3 %maximum_select_fusion = bf16[2,4608,3,128]{3,1,2,0:T(8,128)(2,1)} fusion(bf16[2,2304,3,128]{3,1,2,0:T(8,128)(2,1)} %collective-permute-done.2, bf16[2,2304,3,128]{3,1,2,0:T(8,128)(2,1)} %maximum_select_fusion.1, pred[]{:T(512)S(6)} %eq.18), kind=kLoop, calls=%fused_computation.35 | loop fusion | flops 31850496 | bytes 14155777 | tf_op jit(solution)/shard_map/jit(_where)/select_n | solution.py:151
  292.8 102.5 %while.21 = (s32[]{:T(128)}, f32[3,576]{1,0:T(4,128)S(1)}, f32[3,576]{1,0:T(4,128)S(1)}, f32[3,576,128]{2,1,0:T(8,128)}, s32[]{:T(128)}, /*index=5*/bf16[2,4608,...) while((s32[]{:T(128)}, f32[3,576]{1,0:T(4,128)S(1)}, ...), condition=%wide.region_7.8_spmd.clone.clone, body=%wide.region_4.7_spmd.clone.clone.sunk | while | flops 521231616 | bytes 15596003 | solution.py:95
  293.5 3.9 bitcast_reduce_fusion.2
  300.7 4.7 fusion.72
  306.1 3.9 bitcast_reduce_fusion.2
  313.3 5.0 fusion.72
  318.9 3.9 bitcast_reduce_fusion.2
  326.1 5.0 fusion.72
  331.7 3.9 bitcast_reduce_fusion.2
  339.0 5.0 fusion.72
  344.6 3.9 bitcast_reduce_fusion.2
  351.8 5.0 fusion.72
  357.4 3.9 bitcast_reduce_fusion.2
  364.7 5.0 fusion.72
  370.3 3.9 bitcast_reduce_fusion.2
  377.5 5.0 fusion.72
  383.1 3.9 bitcast_reduce_fusion.2
  390.3 5.0 fusion.72
  397.1 3.8 convolution_convert_fusion
  402.7 80.0 %reduce-scatter.2.cloned.1.call-done = bf16[576,768]{1,0:T(8,128)(2,1)} async-done(((bf16[576,3072]{1,0:T(8,128)(2,1)}), bf16[576,768]{1,0:T(8,128)(2,1)}) %reduce-scatter.2.cloned.1.call-update) | async-done | bytes 884752 | tf_op jit(solution)/shard_map/reduce_scatter | solution.py:162
  485.4 10.7 %all-reduce = (f32[512]{0:T(512)S(1)}, f32[512]{0:T(512)S(1)}) all-reduce(f32[512]{0:T(512)S(1)} %get-tuple-element.267, f32[512]{0:T(512)S(1)} %get-tuple-element.266), channel_id=1, replica_groups=mesh['pair'=2,'seq'=32,'tp'=4] {'tp'}, use_global_device_ids=true, to_apply=%region_12.13 | all-reduce | flops 1024 | bytes 8192 | tf_op jit(solution)/shard_map/psum | solution.py:174
  499.9 48.9 %all-reduce.3.cloned.1.call-done = bf16[512,64]{0,1:T(8,128)(2,1)} async-done(((bf16[512,64]{0,1:T(8,128)(2,1)}), bf16[512,64]{0,1:T(8,128)(2,1)}) %all-reduce.3.cloned.1.call-update) | async-done | bytes 65552 | tf_op jit(solution)/shard_map/psum | solution.py:180
  (117 shorter events, 80.6 us)
Async XLA Ops:
  7.2 389.9 %copy-start = (bf16[384,3072]{1,0:T(8,128)(2,1)S(1)}, bf16[384,3072]{1,0:T(8,128)(2,1)}, u32[]{:S(2)}) copy-start(bf16[384,3072]{1,0:T(8,128)(2,1)} %param.23) | copy-start | bytes 7077892
  7.2 78.7 %all-gather.2.cloned.1.call-start = ((), (), s32[]{:S(2)}) async-start(), calls=%async_computation.1 | async-start | bytes 4423680 | tf_op jit(solution)/shard_map/all_gather | solution.py:119
  7.9 474.8 %reduce-scatter.2.cloned.1.call-start = ((), (), s32[]{:S(2)}) async-start(), calls=%async_computation.2 | async-start | bytes 4423680 | tf_op jit(solution)/shard_map/reduce_scatter | solution.py:162
  8.0 10.3 %copy-start.8 = (f32[128]{0:T(128)S(1)}, f32[128]{0:T(128)}, u32[]{:S(2)}) copy-start(f32[128]{0:T(128)} %param.22) | copy-start | bytes 1540
  8.0 10.4 %copy-start.9 = (f32[128]{0:T(128)S(1)}, f32[128]{0:T(128)}, u32[]{:S(2)}) copy-start(f32[128]{0:T(128)} %param.21) | copy-start | bytes 1540
  8.0 10.6 %copy-start.7 = (s32[3,576]{1,0:T(4,128)S(1)}, s32[3,576]{1,0:T(4,128)}, u32[]{:S(2)}) copy-start(s32[3,576]{1,0:T(4,128)} %param.15) | copy-start | bytes 20740
  85.9 3.3 copy-start.1
  122.5 34.9 %collective-permute-start = (bf16[2,576,3,128]{3,1,2,0:T(8,128)(2,1)}, bf16[2,576,3,128]{3,1,2,0:T(8,128)(2,1)}, u32[]{:S(2)}, u32[]{:S(2)}) collective-permute-start(bf16[2,576,3,128]{3,1,2,0:T(8,128)(2,1)} %pad_maximum_fusion), channel_id=1, source_target_pairs={{0,4},{4,0},{8,12},{12,8},{16,20},{20,16},{24,28},{28,24},{32,36},... | collective-permute-start | bytes 2654216 | tf_op jit(solution)/shard_map/ppermute | solution.py:23
  160.4 39.7 %collective-permute-start.1 = (bf16[2,1152,3,128]{3,1,2,0:T(8,128)(2,1)}, bf16[2,1152,3,128]{3,1,2,0:T(8,128)(2,1)}, u32[]{:S(2)}, u32[]{:S(2)}) collective-permute-start(bf16[2,1152,3,128]{3,1,2,0:T(8,128)(2,1)} %maximum_select_fusion.2), channel_id=1, source_target_pairs={{0,8},{8,0},{4,12},{12,4},{16,24},{24,16},{20,28},{28,20},{32,40},... | collective-permute-start | bytes 5308424 | tf_op jit(solution)/shard_map/ppermute | solution.py:23
  161.0 46.4 %copy-start.11 = (s32[4]{0:T(128)S(1)}, s32[4]{0:T(128)}, u32[]{:S(2)}) copy-start(s32[4]{0:T(128)} %param.16) | copy-start | bytes 52
  161.0 47.0 %copy-start.4 = (bf16[576,3,64,1]{0,3,2,1:T(2,128)(2,1)S(1)}, bf16[576,3,64,1]{0,3,2,1:T(2,128)(2,1)}, u32[]{:S(2)}) copy-start(bf16[576,3,64,1]{0,3,2,1:T(2,128)(2,1)} %get-tuple-element.295) | copy-start | bytes 663556
  161.0 47.0 %copy-start.5 = (bf16[576,3,64,1]{0,3,2,1:T(2,128)(2,1)S(1)}, bf16[576,3,64,1]{0,3,2,1:T(2,128)(2,1)}, u32[]{:S(2)}) copy-start(bf16[576,3,64,1]{0,3,2,1:T(2,128)(2,1)} %get-tuple-element.296) | copy-start | bytes 663556
  205.4 78.2 %collective-permute-start.2 = (bf16[2,2304,3,128]{3,1,2,0:T(8,128)(2,1)}, bf16[2,2304,3,128]{3,1,2,0:T(8,128)(2,1)}, u32[]{:S(2)}, u32[]{:S(2)}) collective-permute-start(bf16[2,2304,3,128]{3,1,2,0:T(8,128)(2,1)} %maximum_select_fusion.1), channel_id=1, source_target_pairs={{0,16},{16,0},{4,20},{20,4},{8,24},{24,8},{12,28},{28,12},{32,48},... | collective-permute-start | bytes 10616840 | tf_op jit(solution)/shard_map/ppermute | solution.py:23
  400.8 81.8 %copy-start.2 = (bf16[576,768]{1,0:T(8,128)(2,1)S(1)}, bf16[576,768]{1,0:T(8,128)(2,1)}, u32[]{:S(2)}) copy-start(bf16[576,768]{1,0:T(8,128)(2,1)} %param.14) | copy-start | bytes 2654212
  400.8 95.3 %copy-start.10 = (bf16[768,64]{0,1:T(8,128)(2,1)S(1)}, bf16[768,64]{0,1:T(8,128)(2,1)}, u32[]{:S(2)}) copy-start(bf16[768,64]{0,1:T(8,128)(2,1)} %param.24) | copy-start | bytes 294916
  400.9 152.8 %copy-start.6 = (f32[256,64]{0,1:T(8,128)S(1)}, f32[256,64]{0,1:T(8,128)}, u32[]{:S(2)}) copy-start(f32[256,64]{0,1:T(8,128)} %param.25) | copy-start | bytes 196612
  400.9 147.9 %all-reduce.3.cloned.1.call-start = ((), (), s32[]{:S(2)}) async-start(), calls=%async_computation.3 | async-start | bytes 131072 | tf_op jit(solution)/shard_map/psum | solution.py:180
  484.1 0.9 copy-start.3
  549.7 4.0 collective-permute-start.3
Sparse Core Ops, SparseCore 0:
  9.8 76.0 all-gather.1
  401.0 81.6 reduce-scatter.1
  499.3 49.4 all-reduce.2
where the time goes:
time: 563 us; the launch traced here: 561 us
  waiting for transfers between devices  338 us (60%)
  matrix products  85.7 us (15%)
  other arithmetic  73.4 us (13%)
  local copies, waits for them, and re-layouts  28.9 us (5%)
  between operations  14.7 us (3%)
  blocking collectives  10.7 us (2%)
  starting transfers between devices  8.84 us (2%)
    ppermute x4, waiting for transfers between devices, swapped(): return lax.ppermute(block, axis, route)  143 us
    reduce_scatter x1, waiting for transfers between devices, on_device(): lax.psum_scatter(partial_out.astype(jnp.bfloat16), 'tp', scatter_dimensio...  80 us
    all_gather x1, waiting for transfers between devices, on_device(): gathered = lax.all_gather(hidden, 'tp', axis=1, tiled=True)  65.6 us
    psum x1, waiting for transfers between devices, on_device(): lax.psum(jnp.dot(final_in, weight, precision=lax.Precision.HIGHEST).astyp...  48.9 us
    dot_general x8, matrix products, fold_piece(): jnp.einsum('hqk,khd->hqd', exps.astype(jnp.bfloat16), key_piece[1], prefe...  39.4 us
    dot_general x8, matrix products, fold_piece(): jnp.einsum('qhd,khd->hqk', queries, key_piece[0], preferred_element_type=...  31.6 us
    reduce_sum x8, other arithmetic, fold_piece(): row_sum = row_sum * decay + jnp.sum(exps, axis=2)  25.9 us
    select_n x3, other arithmetic, on_device(): jnp.where(lower_half, jnp.concatenate([held_keys, far_keys], axis=1), jnp...  17.7 us
  transfers between devices with their start and end apart: 7, of which 7 were waited for; matrix products, arithmetic and copies ran while one was open for 3% of the time, Pallas kernels for 0%

commit v1 on v0

--- a/solution.py
+++ b/solution.py
@@ -116,7 +116,9 @@
     shard_pos = seq_pos % spread
     tp_pos = lax.axis_index("tp")
     local_width = hidden.shape[1]
-    gathered = lax.all_gather(hidden, "tp", axis=1, tiled=True)
+    gathered = jnp.concatenate(
+        lax.all_to_all(jnp.stack([hidden] * lax.axis_size("tp")), "tp", 0, 0), axis=1
+    )
     model_width = gathered.shape[1]
     rows_dev = gathered.shape[0]
     layer_terms = lax.dynamic_index_in_dim(layer_mod, local_seq, 0, keepdims=False)

time: 563 us -> 585 us (1.039)
  local copies, waits for them, and re-layouts: 28.9 us -> 44.3 us
  starting transfers between devices: 8.84 us -> 16.4 us
    all_to_all x0 -> x1, waiting for transfers between devices: none -> 66.8 us  [on_device(): lax.all_to_all(jnp.stack([hidden] * lax.axis_size('tp')), 'tp', 0, 0)]
    all_gather x1 -> x0, waiting for transfers between devices: 65.6 us -> none  [on_device(): gathered = lax.all_gather(hidden, 'tp', axis=1, tiled=True)]
    reduce_scatter x1, waiting for transfers between devices: 80 us -> 67.9 us  [on_device(): lax.psum_scatter(partial_out.astype(jnp.bfloat16), 'tp', scatter_dimensio...]
    convert_element_type x0 -> x2, local copies, waits for them, and re-layouts: none -> 11.9 us  [on_device(): modulate(gathered.astype(jnp.float32), layer_terms[0], layer_terms[1])]
    ppermute x4, waiting for transfers between devices: 143 us -> 151 us  [swapped(): return lax.ppermute(block, axis, route)]
    all_to_all x0 -> x1, starting transfers between devices: none -> 5.89 us  [on_device(): lax.all_to_all(jnp.stack([hidden] * lax.axis_size('tp')), 'tp', 0, 0)]
where the time goes in v1:
time: 585 us; the launch traced here: 583 us
  waiting for transfers between devices  334 us (57%)
  matrix products  85.5 us (15%)
  other arithmetic  76.8 us (13%)
  local copies, waits for them, and re-layouts  44.3 us (8%)
  starting transfers between devices  16.4 us (3%)
  between operations  15 us (3%)
  blocking collectives  10.8 us (2%)
    ppermute x4, waiting for transfers between devices, swapped(): return lax.ppermute(block, axis, route)  151 us
    reduce_scatter x1, waiting for transfers between devices, on_device(): lax.psum_scatter(partial_out.astype(jnp.bfloat16), 'tp', scatter_dimensio...  67.9 us
    all_to_all x1, waiting for transfers between devices, on_device(): lax.all_to_all(jnp.stack([hidden] * lax.axis_size('tp')), 'tp', 0, 0)  66.8 us
    psum x1, waiting for transfers between devices, on_device(): lax.psum(jnp.dot(final_in, weight, precision=lax.Precision.HIGHEST).astyp...  48.9 us
    dot_general x8, matrix products, fold_piece(): jnp.einsum('hqk,khd->hqd', exps.astype(jnp.bfloat16), key_piece[1], prefe...  39.4 us
    dot_general x8, matrix products, fold_piece(): jnp.einsum('qhd,khd->hqk', queries, key_piece[0], preferred_element_type=...  31.6 us
    reduce_sum x8, other arithmetic, fold_piece(): row_sum = row_sum * decay + jnp.sum(exps, axis=2)  25.9 us
    select_n x3, other arithmetic, on_device(): jnp.where(lower_half, jnp.concatenate([held_keys, far_keys], axis=1), jnp...  17.7 us
  transfers between devices with their start and end apart: 7, of which 7 were waited for; matrix products, arithmetic and copies ran while one was open for 3% of the time, Pallas kernels for 0%

profile of v1, /device:TPU:2, one launch (start us, length us, event | category | flops | bytes accessed | tf_op | source)
XLA Modules:
  0.0 583.1 jit_solution(3870859374849827114)
XLA Ops:
  10.6 5.9 %all-to-all-start = ((bf16[4,576,768]{2,1,0:T(8,128)(2,1)}), bf16[4,576,768]{2,1,0:T(8,128)(2,1)}, u32[]{:S(2)}, u32[]{:S(2)}) async-start(bf16[4,576,768]{2,1,0:T(8,128)(2,1)} %stack.10), calls=%async_computation | async-start | bytes 7077888 | tf_op jit(solution)/shard_map/all_to_all | solution.py:120
  17.5 10.3 %copy.32 = bf16[3072,3,384]{0,2,1:T(8,128)(2,1)} copy(bf16[3072,3,384]{2,0,1:T(8,128)(2,1)} %param.20) | data formatting | bytes 14155776 | tf_op args[6]
  28.9 66.8 %all-to-all-done = bf16[4,576,768]{2,1,0:T(8,128)(2,1)} async-done(((bf16[4,576,768]{2,1,0:T(8,128)(2,1)}), bf16[4,576,768]{2,1,0:T(8,128)(2,1)}, u32[]{:S(2)}, u32[]{:S(2)}) %all-to-all-start) | async-done | bytes 3538976 | tf_op jit(solution)/shard_map/all_to_all | solution.py:120
  102.4 4.6 copy.31
  107.0 7.3 %reshape.299 = bf16[576,3072,1,1]{1,0,2,3:T(8,128)(2,1)} reshape(bf16[576,4,768]{2,1,0:T(4,128)(2,1)} %copy.31) | data formatting | bytes 7077888 | tf_op jit(solution)/shard_map/convert_element_type | solution.py:126
  114.3 7.7 %fusion.26 = f32[576,3,3,128]{3,0,2,1:T(8,128)S(1)} fusion(bf16[3,3,128,3072]{3,2,1,0:T(8,128)(2,1)} %bitcast.66, bf16[576,3072,1,1]{1,0,2,3:T(8,128)(2,1)} %reshape.299), kind=kOutput, calls=%fused_computation.39 | convolution fusion | flops 4076863488 | bytes 13271040 | tf_op jit(solution)/shard_map/dot_general | solution.py:132
  147.3 6.2 %collective-permute-start = (bf16[2,576,3,128]{3,1,2,0:T(8,128)(2,1)}, bf16[2,576,3,128]{3,1,2,0:T(8,128)(2,1)}, u32[]{:S(2)}, u32[]{:S(2)}) collective-permute-start(bf16[2,576,3,128]{3,1,2,0:T(8,128)(2,1)} %pad_maximum_fusion), channel_id=1, source_target_pairs={{0,4},{4,0},{8,12},{12,8},{16,20},{20,16},{24,28},{28,24},{32,36},... | collective-permute-start | bytes 2654216 | tf_op jit(solution)/shard_map/ppermute | solution.py:23
  153.6 38.6 %collective-permute-done = bf16[2,576,3,128]{3,1,2,0:T(8,128)(2,1)} collective-permute-done((bf16[2,576,3,128]{3,1,2,0:T(8,128)(2,1)}, bf16[2,576,3,128]{3,1,2,0:T(8,128)(2,1)}, u32[]{:S(2)}, u32[]{:S(2)}) %collective-permute-start) | collective-permute-done | bytes 884768 | tf_op jit(solution)/shard_map/ppermute | solution.py:23
  195.8 38.7 %collective-permute-done.1 = bf16[2,1152,3,128]{3,1,2,0:T(8,128)(2,1)} collective-permute-done((bf16[2,1152,3,128]{3,1,2,0:T(8,128)(2,1)}, bf16[2,1152,3,128]{3,1,2,0:T(8,128)(2,1)}, u32[]{:S(2)}, u32[]{:S(2)}) %collective-permute-start.1) | collective-permute-done | bytes 1769504 | tf_op jit(solution)/shard_map/ppermute | solution.py:23
  234.5 5.3 maximum_select_fusion.1
  246.1 71.4 %collective-permute-done.2 = bf16[2,2304,3,128]{3,1,2,0:T(8,128)(2,1)} collective-permute-done((bf16[2,2304,3,128]{3,1,2,0:T(8,128)(2,1)}, bf16[2,2304,3,128]{3,1,2,0:T(8,128)(2,1)}, u32[]{:S(2)}, u32[]{:S(2)}) %collective-permute-start.2) | collective-permute-done | bytes 3538976 | tf_op jit(solution)/shard_map/ppermute | solution.py:23
  317.5 9.3 %maximum_select_fusion = bf16[2,4608,3,128]{3,1,2,0:T(8,128)(2,1)} fusion(bf16[2,2304,3,128]{3,1,2,0:T(8,128)(2,1)} %collective-permute-done.2, bf16[2,2304,3,128]{3,1,2,0:T(8,128)(2,1)} %maximum_select_fusion.1, pred[]{:T(512)S(6)} %eq.18), kind=kLoop, calls=%fused_computation.35 | loop fusion | flops 31850496 | bytes 14155777 | tf_op jit(solution)/shard_map/jit(_where)/select_n | solution.py:153
  326.8 102.5 %while.21 = (s32[]{:T(128)}, f32[3,576]{1,0:T(4,128)S(1)}, f32[3,576]{1,0:T(4,128)S(1)}, f32[3,576,128]{2,1,0:T(8,128)}, s32[]{:T(128)}, /*index=5*/bf16[2,4608,...) while((s32[]{:T(128)}, f32[3,576]{1,0:T(4,128)S(1)}, ...), condition=%wide.region_7.8_spmd.clone.clone, body=%wide.region_4.7_spmd.clone.clone.sunk | while | flops 521231616 | bytes 15596003 | solution.py:95
  327.5 3.9 bitcast_reduce_fusion.2
  334.7 4.7 fusion.69
  340.0 3.9 bitcast_reduce_fusion.2
  347.3 5.0 fusion.69
  352.9 3.9 bitcast_reduce_fusion.2
  360.1 5.0 fusion.69
  365.7 3.9 bitcast_reduce_fusion.2
  372.9 5.0 fusion.69
  378.6 3.9 bitcast_reduce_fusion.2
  385.8 5.0 fusion.69
  391.4 3.9 bitcast_reduce_fusion.2
  398.6 5.0 fusion.69
  404.3 3.9 bitcast_reduce_fusion.2
  411.5 5.0 fusion.69
  417.1 3.9 bitcast_reduce_fusion.2
  424.3 5.0 fusion.69
  436.7 67.9 %reduce-scatter.2.cloned.1.call-done = bf16[576,768]{1,0:T(8,128)(2,1)} async-done(((bf16[576,3072]{1,0:T(8,128)(2,1)}), bf16[576,768]{1,0:T(8,128)(2,1)}) %reduce-scatter.2.cloned.1.call-update) | async-done | bytes 884752 | tf_op jit(solution)/shard_map/reduce_scatter | solution.py:164
  507.3 10.8 %all-reduce = (f32[512]{0:T(512)S(1)}, f32[512]{0:T(512)S(1)}) all-reduce(f32[512]{0:T(512)S(1)} %get-tuple-element.281, f32[512]{0:T(512)S(1)} %get-tuple-element.280), channel_id=1, replica_groups=mesh['pair'=2,'seq'=32,'tp'=4] {'tp'}, use_global_device_ids=true, to_apply=%region_12.13 | all-reduce | flops 1024 | bytes 8192 | tf_op jit(solution)/shard_map/psum | solution.py:176
  521.8 48.9 %all-reduce.3.cloned.1.call-done = bf16[512,64]{0,1:T(8,128)(2,1)} async-done(((bf16[512,64]{0,1:T(8,128)(2,1)}), bf16[512,64]{0,1:T(8,128)(2,1)}) %all-reduce.3.cloned.1.call-update) | async-done | bytes 65552 | tf_op jit(solution)/shard_map/psum | solution.py:182
  (120 shorter events, 97.2 us)
Async XLA Ops:
  7.2 423.9 %copy-start = (bf16[384,3072]{1,0:T(8,128)(2,1)S(1)}, bf16[384,3072]{1,0:T(8,128)(2,1)}, u32[]{:S(2)}) copy-start(bf16[384,3072]{1,0:T(8,128)(2,1)} %param.23) | copy-start | bytes 7077892
  10.6 85.1 %all-to-all-start = ((bf16[4,576,768]{2,1,0:T(8,128)(2,1)}), bf16[4,576,768]{2,1,0:T(8,128)(2,1)}, u32[]{:S(2)}, u32[]{:S(2)}) async-start(bf16[4,576,768]{2,1,0:T(8,128)(2,1)} %stack.10), calls=%async_computation | async-start | bytes 7077888 | tf_op jit(solution)/shard_map/all_to_all | solution.py:120
  16.5 488.1 %reduce-scatter.2.cloned.1.call-start = ((), (), s32[]{:S(2)}) async-start(), calls=%async_computation.2 | async-start | bytes 4423680 | tf_op jit(solution)/shard_map/reduce_scatter | solution.py:164
  17.4 10.3 %copy-start.7 = (f32[128]{0:T(128)S(1)}, f32[128]{0:T(128)}, u32[]{:S(2)}) copy-start(f32[128]{0:T(128)} %param.22) | copy-start | bytes 1540
  17.4 10.4 %copy-start.8 = (f32[128]{0:T(128)S(1)}, f32[128]{0:T(128)}, u32[]{:S(2)}) copy-start(f32[128]{0:T(128)} %param.21) | copy-start | bytes 1540
  17.5 10.6 %copy-start.6 = (s32[3,576]{1,0:T(4,128)S(1)}, s32[3,576]{1,0:T(4,128)}, u32[]{:S(2)}) copy-start(s32[3,576]{1,0:T(4,128)} %param.15) | copy-start | bytes 20740
  147.3 44.8 %collective-permute-start = (bf16[2,576,3,128]{3,1,2,0:T(8,128)(2,1)}, bf16[2,576,3,128]{3,1,2,0:T(8,128)(2,1)}, u32[]{:S(2)}, u32[]{:S(2)}) collective-permute-start(bf16[2,576,3,128]{3,1,2,0:T(8,128)(2,1)} %pad_maximum_fusion), channel_id=1, source_target_pairs={{0,4},{4,0},{8,12},{12,8},{16,20},{20,16},{24,28},{28,24},{32,36},... | collective-permute-start | bytes 2654216 | tf_op jit(solution)/shard_map/ppermute | solution.py:23
  195.3 39.2 %collective-permute-start.1 = (bf16[2,1152,3,128]{3,1,2,0:T(8,128)(2,1)}, bf16[2,1152,3,128]{3,1,2,0:T(8,128)(2,1)}, u32[]{:S(2)}, u32[]{:S(2)}) collective-permute-start(bf16[2,1152,3,128]{3,1,2,0:T(8,128)(2,1)} %maximum_select_fusion.2), channel_id=1, source_target_pairs={{0,8},{8,0},{4,12},{12,4},{16,24},{24,16},{20,28},{28,20},{32,40},... | collective-permute-start | bytes 5308424 | tf_op jit(solution)/shard_map/ppermute | solution.py:23
  195.8 46.1 %copy-start.10 = (s32[4]{0:T(128)S(1)}, s32[4]{0:T(128)}, u32[]{:S(2)}) copy-start(s32[4]{0:T(128)} %param.16) | copy-start | bytes 52
  195.8 46.7 %copy-start.3 = (bf16[576,3,64,1]{0,3,2,1:T(2,128)(2,1)S(1)}, bf16[576,3,64,1]{0,3,2,1:T(2,128)(2,1)}, u32[]{:S(2)}) copy-start(bf16[576,3,64,1]{0,3,2,1:T(2,128)(2,1)} %get-tuple-element.311) | copy-start | bytes 663556
  195.8 46.7 %copy-start.4 = (bf16[576,3,64,1]{0,3,2,1:T(2,128)(2,1)S(1)}, bf16[576,3,64,1]{0,3,2,1:T(2,128)(2,1)}, u32[]{:S(2)}) copy-start(bf16[576,3,64,1]{0,3,2,1:T(2,128)(2,1)} %get-tuple-element.312) | copy-start | bytes 663556
  239.7 77.7 %collective-permute-start.2 = (bf16[2,2304,3,128]{3,1,2,0:T(8,128)(2,1)}, bf16[2,2304,3,128]{3,1,2,0:T(8,128)(2,1)}, u32[]{:S(2)}, u32[]{:S(2)}) collective-permute-start(bf16[2,2304,3,128]{3,1,2,0:T(8,128)(2,1)} %maximum_select_fusion.1), channel_id=1, source_target_pairs={{0,16},{16,0},{4,20},{20,4},{8,24},{24,8},{12,28},{28,12},{32,48},... | collective-permute-start | bytes 10616840 | tf_op jit(solution)/shard_map/ppermute | solution.py:23
  434.8 69.8 %copy-start.1 = (bf16[576,768]{1,0:T(8,128)(2,1)S(1)}, bf16[576,768]{1,0:T(8,128)(2,1)}, u32[]{:S(2)}) copy-start(bf16[576,768]{1,0:T(8,128)(2,1)} %param.14) | copy-start | bytes 2654212
  434.8 83.2 %copy-start.9 = (bf16[768,64]{0,1:T(8,128)(2,1)S(1)}, bf16[768,64]{0,1:T(8,128)(2,1)}, u32[]{:S(2)}) copy-start(bf16[768,64]{0,1:T(8,128)(2,1)} %param.24) | copy-start | bytes 294916
  434.8 140.8 %copy-start.5 = (f32[256,64]{0,1:T(8,128)S(1)}, f32[256,64]{0,1:T(8,128)}, u32[]{:S(2)}) copy-start(f32[256,64]{0,1:T(8,128)} %param.25) | copy-start | bytes 196612
  434.9 135.9 %all-reduce.3.cloned.1.call-start = ((), (), s32[]{:S(2)}) async-start(), calls=%async_computation.3 | async-start | bytes 131072 | tf_op jit(solution)/shard_map/psum | solution.py:182
  506.0 0.9 copy-start.2
  571.6 4.0 collective-permute-start.3
Sparse Core Ops, SparseCore 0:
  435.0 69.5 reduce-scatter.1
  521.2 49.4 all-reduce.2
